TPU v7x, 32 devices: a whole 2x2x4 slice. The times are simulated.
32 devices in a mesh: band: 16 (over z, x, core), chan: 2 (over y).
Axes of the slice: x: 2, y: 2, z: 4, core: 2. Of those that a mesh axis runs over, the one named last changes fastest.
Arguments:
- features: bfloat16 [256, 64, 1024], P('chan', 'band'), may hold values from -6 to 6
- depth_kernel: bfloat16 [3, 9, 256], P(None, None, 'chan'), may hold values from -2 to 2
- pointwise: bfloat16 [4, 256, 256], P(None, 'chan'), may hold values from -0.25 to 0.25
- cotangent: bfloat16 [256, 64, 1024], P('chan', 'band'), may hold values from -6 to 6
Outputs:
- output: bfloat16 [256, 64, 1024], P('chan', 'band')
- grad_input: float32 [256, 64, 1024], P('chan', 'band')
- grad_depth: float32 [3, 9, 256], P(None, None, 'chan')
- grad_point: float32 [4, 256, 256], P(None, 'chan')
All inputs are finite; a program needn't handle non-finite values.
Results may differ from a plain program's by a relative error of at most 0.0057.
Values may be sent and summed in bfloat16 or wider, within the bound.
No kernel may reach another device: no remote copies, remote signals or barrier semaphores. Data moves between devices by JAX's collectives and lax.ppermute only.
A program may use at most 128 MiB of HBM per device.

v0:
```python
import jax
import jax.numpy as jnp
from jax import lax
from jax.sharding import PartitionSpec as P

GSCALE = 1024
dilations = (6, 12, 18)


def shifted(block, axis, distance):
    devices = range(lax.axis_size(axis))
    route = [(i - distance, i) for i in devices if i - distance in devices]
    if not route:
        return jnp.zeros_like(block)
    return lax.ppermute(block, axis, route)


def from_device(block, ahead):
    return block if ahead == 0 else shifted(block, "band", -ahead)


def rows_at(field, offset):
    height = field.shape[1]
    ahead, start = divmod(offset, height)
    if start == 0:
        return from_device(field, ahead)
    return jnp.concatenate(
        [from_device(field[:, start:], ahead), from_device(field[:, :start], ahead + 1)], axis=1
    )


def local(features, depth_kernel, pointwise, cotangent):
    kernel = depth_kernel.astype(jnp.float32)
    feat_rows = {0: features}
    for spacing in dilations:
        for side in (-1, 1):
            feat_rows[side * spacing] = rows_at(features, side * spacing)
    feat_rows = {k: v.astype(jnp.float32) for k, v in feat_rows.items()}
    branches = [features]
    for which, spacing in enumerate(dilations):
        total = jnp.zeros(features.shape, jnp.float32)
        for tap_index in range(9):
            row_step = tap_index // 3 - 1
            col_step = tap_index % 3 - 1
            total = total + kernel[which, tap_index][:, None, None] * jnp.roll(
                feat_rows[row_step * spacing], -col_step * spacing, axis=-1
            )
        branches.append(total.astype(jnp.bfloat16))
    stacked = jnp.stack(branches)
    output = lax.psum_scatter(
        jnp.einsum("bchw,bco->ohw", stacked, pointwise, preferred_element_type=jnp.float32).astype(
            jnp.bfloat16
        ),
        "chan",
        scatter_dimension=0,
        tiled=True,
    )
    cot_full = lax.all_gather(cotangent, "chan", axis=0, tiled=True)
    grad_sum = jnp.einsum("bco,ohw->bchw", pointwise, cot_full, preferred_element_type=jnp.float32)
    point_local = jnp.einsum("bchw,ohw->bco", stacked, cot_full, preferred_element_type=jnp.float32)
    grad_branches = grad_sum.astype(jnp.bfloat16)
    grad_input = grad_branches[0].astype(jnp.float32)
    depth_rows = []
    for which, spacing in enumerate(dilations):
        grad_field = grad_branches[which + 1]
        grad_f = grad_field.astype(jnp.float32)
        grad_rows = {0: grad_f}
        for side in (-1, 1):
            grad_rows[side * spacing] = rows_at(grad_field, side * spacing).astype(jnp.float32)
        tap_rows = []
        for tap_index in range(9):
            row_step = tap_index // 3 - 1
            col_step = tap_index % 3 - 1
            grad_input = grad_input + kernel[which, tap_index][:, None, None] * jnp.roll(
                grad_rows[-row_step * spacing], col_step * spacing, axis=-1
            )
            tap_rows.append(
                jnp.sum(
                    grad_f * jnp.roll(feat_rows[row_step * spacing], -col_step * spacing, axis=-1),
                    axis=(1, 2),
                )
            )
        depth_rows.append(jnp.stack(tap_rows))
    depth_local = jnp.stack(depth_rows)
    flat = jnp.concatenate([depth_local.reshape(-1), point_local.reshape(-1)])
    flat = lax.psum(flat, "band")
    depth_total = flat[: depth_local.size].reshape(depth_local.shape)
    point_total = flat[depth_local.size :].reshape(point_local.shape)
    return (output, grad_input, depth_total / GSCALE, point_total / GSCALE)


def solution(mesh):
    return jax.shard_map(
        local,
        mesh=mesh,
        in_specs=(
            P("chan", "band", None),
            P(None, None, "chan"),
            P(None, "chan", None),
            P("chan", "band", None),
        ),
        out_specs=(
            P("chan", "band", None),
            P("chan", "band", None),
            P(None, None, "chan"),
            P(None, "chan", None),
        ),
        check_vma=False,
    )
```

profile of v0, /device:TPU:0, one launch (start us, length us, event | category | flops | bytes accessed | tf_op | source)
XLA Modules:
  0.0 347.8 jit_solution(9047192822826043685)
XLA Ops:
  11.5 5.1 %collective-permute-start.6 = (bf16[128,2,1024]{0,2,1:T(8,128)(2,1)}, bf16[128,2,1024]{0,2,1:T(8,128)(2,1)S(1)}, u32[]{:S(2)}, u32[]{:S(2)}) collective-permute-start(bf16[128,2,1024]{0,2,1:T(8,128)(2,1)} %get-tuple-element.125), channel_id=1, source_target_pairs={{0,10},{2,12},{4,14},{6,16},{8,18},{10,20},{12,22},{14,24},{16,26}... | collective-permute-start | bytes 1572872 | tf_op jit(solution)/shard_map/ppermute | solution.py:15
  17.9 7.0 %collective-permute-start = (bf16[128,2,1024]{0,2,1:T(8,128)(2,1)}, bf16[128,2,1024]{0,2,1:T(8,128)(2,1)}, u32[]{:S(2)}, u32[]{:S(2)}) collective-permute-start(bf16[128,2,1024]{0,2,1:T(8,128)(2,1)} %get-tuple-element.125), channel_id=1, source_target_pairs={{0,4},{2,6},{4,8},{6,10},{8,12},{10,14},{12,16},{14,18},{16,20},{1... | collective-permute-start | bytes 1572872 | tf_op jit(solution)/shard_map/ppermute | solution.py:15
  34.1 7.1 %collective-permute-done.7 = bf16[128,2,1024]{0,2,1:T(8,128)(2,1)S(1)} collective-permute-done((bf16[128,2,1024]{0,2,1:T(8,128)(2,1)}, bf16[128,2,1024]{0,2,1:T(8,128)(2,1)S(1)}, u32[]{:S(2)}, u32[]{:S(2)}) %collective-permute-start.7) | collective-permute-done | bytes 524320 | tf_op jit(solution)/shard_map/ppermute | solution.py:15
  50.4 19.0 %collective-permute-start.4 = (bf16[128,4,1024]{0,2,1:T(8,128)(2,1)S(1)}, bf16[128,4,1024]{0,2,1:T(8,128)(2,1)S(1)}, u32[]{:S(2)}, u32[]{:S(2)}) collective-permute-start(bf16[128,4,1024]{0,2,1:T(8,128)(2,1)S(1)} %copy.35), channel_id=1, source_target_pairs={{0,6},{2,8},{4,10},{6,12},{8,14},{10,16},{12,18},{14,20},{16,22},{... | collective-permute-start | bytes 3145736 | tf_op jit(solution)/shard_map/ppermute | solution.py:15
  74.7 7.1 %fusion.75 = bf16[1,128,4,1024]{1,3,0,2:T(8,128)(2,1)} fusion(f32[128,4,18]{0,2,1:T(8,128)S(1)} %get-tuple-element.90, f32[128,4,1006]{0,2,1:T(8,128)} %get-tuple-element.92, f32[128]{0:T(128)S(1)} %get-tuple-element.128, f32[128]{0:T(128)S(1)} %get-tuple-element.129, f32[128,4,1006]{0,2,1:T(8,128)} %get-tuple-element.91, ...), kind=kLoop, calls=%fused_computation.159 | loop fusion | flops 15204352 | bytes 16781824 | tf_op jit(solution)/shard_map/stack | solution.py:49
  82.0 5.8 %fusion.77 = bf16[1,128,4,1024]{1,3,0,2:T(8,128)(2,1)} fusion(f32[128,4,6]{0,2,1:T(8,128)S(1)} %get-tuple-element.82, f32[128,4,1018]{0,2,1:T(8,128)S(1)} %get-tuple-element.84, f32[128]{0:T(128)} %get-tuple-element.147, f32[128]{0:T(128)} %get-tuple-element.148, f32[128,4,1018]{0,2,1:T(8,128)S(1)} %get-tuple-element.83, ...), kind=kLoop, calls=%fused_computation.161 | loop fusion | flops 15204352 | bytes 16781824 | tf_op jit(solution)/shard_map/stack | solution.py:49
  87.9 9.6 %collective-permute-done.4 = bf16[128,4,1024]{0,2,1:T(8,128)(2,1)S(1)} collective-permute-done((bf16[128,4,1024]{0,2,1:T(8,128)(2,1)S(1)}, bf16[128,4,1024]{0,2,1:T(8,128)(2,1)S(1)}, u32[]{:S(2)}, u32[]{:S(2)}) %collective-permute-start.4) | collective-permute-done | bytes 1048608 | tf_op jit(solution)/shard_map/ppermute | solution.py:15
  101.3 4.3 %fusion.76 = bf16[1,128,4,1024]{1,3,0,2:T(8,128)(2,1)} fusion(f32[128,4,12]{0,2,1:T(8,128)S(1)} %get-tuple-element.118, f32[128,4,1012]{0,2,1:T(8,128)S(1)} %get-tuple-element.120, f32[128]{0:T(128)S(1)} %copy-done.97, bf16[128,4,1024]{0,2,1:T(8,128)(2,1)S(1)} %collective-permute-done.5, f32[128]{0:T(128)S(1)} %copy-done.98, ...), kind=kLoop, calls=%fused_computation.160 | loop fusion | flops 14155776 | bytes 16781824 | tf_op jit(solution)/shard_map/stack | solution.py:49
  105.7 3.0 convolution_convert_fusion
  109.2 5.9 %fusion.47 = (f32[128]{0:T(128)}, f32[128]{0:T(128)}, f32[128]{0:T(128)}, f32[128]{0:T(128)}, f32[128]{0:T(128)}, /*index=5*/f32[128]{0:T(128)}) fusion(f32[128,4,1018]{0,2,1:T(8,128)S(1)} %copy-done.15, f32[128,4,6]{0,2,1:T(8,128)S(1)} %copy-done.84, bf16[4,128,4,1024]{1,3,2,0:T(8,128)(2,1)S(1)} %convolution_convert_fusion, ...), kind=kLoop, calls=%fused_computation.83 | loop fusion | flops 10484992 | bytes 14683136 | tf_op jit(solution)/shard_map/reduce_sum | solution.py:78
  118.5 4.5 %fusion.48 = (f32[128]{0:T(128)}, f32[128]{0:T(128)}, f32[128]{0:T(128)}, f32[128]{0:T(128)}, f32[128]{0:T(128)}, /*index=5*/f32[128]{0:T(128)}, f32[128]{0:T(128)}) fusion(bf16[128,2,1024]{0,2,1:T(8,128)(2,1)S(1)} %copy-done.41, bf16[128,2,1024]{0,2,1:T(8,128)(2,1)} %collective-permute-done.2, bf16[4,128,4,1024]{1,3,2,0:T(8,128)(2,1)S(1)} %convolution_convert_fusion, ...), kind=kLoop, calls=%fused_computation.84 | loop fusion | flops 13630592 | bytes 13635072 | tf_op jit(solution)/shard_map/reduce_sum | solution.py:78
  123.1 4.9 %fusion.45 = (f32[128]{0:T(128)}, f32[128]{0:T(128)}, f32[128]{0:T(128)}, f32[128]{0:T(128)}, f32[128]{0:T(128)}, /*index=5*/f32[128]{0:T(128)}, f32[128]{0:T(128)}, f32[128]{0:T(128)}) fusion(bf16[128,4,1024]{0,2,1:T(8,128)(2,1)S(1)} %copy.35, bf16[4,128,4,1024]{1,3,2,0:T(8,128)(2,1)S(1)} %convolution_convert_fusion, f32[128,4,6]{0,2,1:T(8,128)S(1)} %copy-done.77, ...), kind=kLoop, calls=%fused_computation.81 | loop fusion | flops 13630464 | bytes 13635584 | tf_op jit(solution)/shard_map/reduce_sum | solution.py:78
  130.5 6.4 %fusion.49 = (f32[128]{0:T(128)}, f32[128]{0:T(128)}, f32[128]{0:T(128)}, f32[128]{0:T(128)}, f32[128]{0:T(128)}, /*index=5*/f32[128]{0:T(128)}) fusion(f32[128,4,6]{0,2,1:T(8,128)} %copy-done.78, f32[128,4,1018]{0,2,1:T(8,128)S(1)} %copy-done.13, bf16[4,128,4,1024]{1,3,2,0:T(8,128)(2,1)} %copy-done.2, f32[128,4,18]{0,2,1:T(8,128)} %copy-done.57, ...), kind=kLoop, calls=%fused_computation.85 | loop fusion | flops 11009280 | bytes 13634560 | tf_op jit(solution)/shard_map/reduce_sum | solution.py:78
  142.4 3.1 bitcast_convert_fusion
  145.5 3.0 copy.56
  148.5 3.9 %fusion.84 = (f32[128,4,1024]{0,2,1:T(8,128)S(1)}, f32[128,4,1024]{0,2,1:T(8,128)S(1)}, f32[128,4,1024]{0,2,1:T(8,128)S(1)}, bf16[128,4,1024]{0,2,1:T(8,128)(2,1...) fusion(bf16[4,128,4,1024]{1,3,2,0:T(8,128)(2,1)} %copy-done.2), kind=kLoop, calls=%fused_computation.199 | loop fusion | flops 1572864 | bytes 12582912 | tf_op jit(solution)/shard_map/convert_element_type | solution.py:66
  153.5 20.2 %collective-permute-start.18 = (bf16[128,2,1024]{0,2,1:T(8,128)(2,1)}, bf16[128,2,1024]{0,2,1:T(8,128)(2,1)S(1)}, u32[]{:S(2)}, u32[]{:S(2)}) collective-permute-start(bf16[128,2,1024]{0,2,1:T(8,128)(2,1)} %get-tuple-element.93), channel_id=1, source_target_pairs={{0,10},{2,12},{4,14},{6,16},{8,18},{10,20},{12,22},{14,24},{16,26}... | collective-permute-start | bytes 1572872 | tf_op jit(solution)/shard_map/ppermute | solution.py:15
  175.0 5.6 %collective-permute-start.19 = (bf16[128,2,1024]{0,2,1:T(8,128)(2,1)}, bf16[128,2,1024]{0,2,1:T(8,128)(2,1)S(1)}, u32[]{:S(2)}, u32[]{:S(2)}) collective-permute-start(bf16[128,2,1024]{0,2,1:T(8,128)(2,1)} %get-tuple-element.94), channel_id=1, source_target_pairs={{0,8},{2,10},{4,12},{6,14},{8,16},{10,18},{12,20},{14,22},{16,24},... | collective-permute-start | bytes 1572872 | tf_op jit(solution)/shard_map/ppermute | solution.py:15
  192.9 66.5 %all-reduce.2.cloned.1.call-done = f32[134528]{0:T(1024)} async-done(((f32[134528]{0:T(1024)}), f32[134528]{0:T(1024)}) %all-reduce.2.cloned.1.call-update) | async-done | bytes 538128 | tf_op jit(solution)/shard_map/psum | solution.py:86
  264.1 3.1 collective-permute-start.13
  271.0 6.0 %collective-permute-start.15 = (bf16[128,4,1024]{0,2,1:T(8,128)(2,1)S(1)}, bf16[128,4,1024]{0,2,1:T(8,128)(2,1)S(1)}, u32[]{:S(2)}, u32[]{:S(2)}) collective-permute-start(bf16[128,4,1024]{0,2,1:T(8,128)(2,1)S(1)} %copy-done.54), channel_id=1, source_target_pairs={{0,6},{2,8},{4,10},{6,12},{8,14},{10,16},{12,18},{14,20},{16,22},{... | collective-permute-start | bytes 3145736 | tf_op jit(solution)/shard_map/ppermute | solution.py:15
  280.7 4.8 %collective-permute-done.11 = bf16[128,2,1024]{0,2,1:T(8,128)(2,1)S(1)} collective-permute-done((bf16[128,2,1024]{0,2,1:T(8,128)(2,1)}, bf16[128,2,1024]{0,2,1:T(8,128)(2,1)S(1)}, u32[]{:S(2)}, u32[]{:S(2)}) %collective-permute-start.11) | collective-permute-done | bytes 524320 | tf_op jit(solution)/shard_map/ppermute | solution.py:15
  288.3 24.8 %collective-permute-done.15 = bf16[128,4,1024]{0,2,1:T(8,128)(2,1)S(1)} collective-permute-done((bf16[128,4,1024]{0,2,1:T(8,128)(2,1)S(1)}, bf16[128,4,1024]{0,2,1:T(8,128)(2,1)S(1)}, u32[]{:S(2)}, u32[]{:S(2)}) %collective-permute-start.15) | collective-permute-done | bytes 1048608 | tf_op jit(solution)/shard_map/ppermute | solution.py:15
  320.4 15.6 %fusion.40 = f32[128,4,1024]{0,2,1:T(8,128)S(1)} fusion(f32[128,4,6]{0,2,1:T(8,128)S(1)} %get-tuple-element.74, f32[128,4,1018]{0,2,1:T(8,128)S(1)} %get-tuple-element.76, f32[128,4,1018]{0,2,1:T(8,128)S(1)} %get-tuple-element.75, f32[128,4,6]{0,2,1:T(8,128)S(1)} %get-tuple-element.73, f32[128,4,6]{0,2,1:T(8,128)S(1)} %get-tuple-element.70, ...), kind=kLoop, calls=%fused_computation.76 | loop fusion | flops 45088768 | bytes 50345472 | tf_op jit(solution)/shard_map/add | solution.py:74
  (317 shorter events, 86.1 us)
Async XLA Ops:
  7.2 98.4 %copy-start = (bf16[4,128,256]{2,1,0:T(8,128)(2,1)S(1)}, bf16[4,128,256]{2,1,0:T(8,128)(2,1)}, u32[]{:S(2)}) copy-start(bf16[4,128,256]{2,1,0:T(8,128)(2,1)} %param.6) | copy-start | bytes 786436
  7.2 98.4 %all-gather.2.cloned.1.call-start = ((), (), s32[]{:S(2)}) async-start(), calls=%async_computation.1 | async-start | bytes 3145728 | tf_op jit(solution)/shard_map/all_gather | solution.py:58
  10.2 34.8 %collective-permute-start.8 = (bf16[128,2,1024]{0,2,1:T(8,128)(2,1)}, bf16[128,2,1024]{0,2,1:T(8,128)(2,1)S(1)}, u32[]{:S(2)}, u32[]{:S(2)}) collective-permute-start(bf16[128,2,1024]{0,2,1:T(8,128)(2,1)} %get-tuple-element.125), channel_id=1, source_target_pairs={{8,0},{10,2},{12,4},{14,6},{16,8},{18,10},{20,12},{22,14},{24,16},... | collective-permute-start | bytes 1572872 | tf_op jit(solution)/shard_map/ppermute | solution.py:15
  11.5 21.3 %collective-permute-start.6 = (bf16[128,2,1024]{0,2,1:T(8,128)(2,1)}, bf16[128,2,1024]{0,2,1:T(8,128)(2,1)S(1)}, u32[]{:S(2)}, u32[]{:S(2)}) collective-permute-start(bf16[128,2,1024]{0,2,1:T(8,128)(2,1)} %get-tuple-element.125), channel_id=1, source_target_pairs={{0,10},{2,12},{4,14},{6,16},{8,18},{10,20},{12,22},{14,24},{16,26}... | collective-permute-start | bytes 1572872 | tf_op jit(solution)/shard_map/ppermute | solution.py:15
  16.6 33.8 %collective-permute-start.2 = (bf16[128,2,1024]{0,2,1:T(8,128)(2,1)}, bf16[128,2,1024]{0,2,1:T(8,128)(2,1)}, u32[]{:S(2)}, u32[]{:S(2)}) collective-permute-start(bf16[128,2,1024]{0,2,1:T(8,128)(2,1)} %get-tuple-element.125), channel_id=1, source_target_pairs={{2,0},{4,2},{6,4},{8,6},{10,8},{12,10},{14,12},{16,14},{18,16},{20... | collective-permute-start | bytes 1572872 | tf_op jit(solution)/shard_map/ppermute | solution.py:15
  17.9 53.2 %collective-permute-start = (bf16[128,2,1024]{0,2,1:T(8,128)(2,1)}, bf16[128,2,1024]{0,2,1:T(8,128)(2,1)}, u32[]{:S(2)}, u32[]{:S(2)}) collective-permute-start(bf16[128,2,1024]{0,2,1:T(8,128)(2,1)} %get-tuple-element.125), channel_id=1, source_target_pairs={{0,4},{2,6},{4,8},{6,10},{8,12},{10,14},{12,16},{14,18},{16,20},{1... | collective-permute-start | bytes 1572872 | tf_op jit(solution)/shard_map/ppermute | solution.py:15
  26.3 233.1 %all-reduce.2.cloned.1.call-start = ((), (), s32[]{:S(2)}) async-start(), calls=%async_computation.2 | async-start | bytes 1081344 | tf_op jit(solution)/shard_map/psum | solution.py:86
  26.3 14.9 %collective-permute-start.7 = (bf16[128,2,1024]{0,2,1:T(8,128)(2,1)}, bf16[128,2,1024]{0,2,1:T(8,128)(2,1)S(1)}, u32[]{:S(2)}, u32[]{:S(2)}) collective-permute-start(bf16[128,2,1024]{0,2,1:T(8,128)(2,1)} %get-tuple-element.126), channel_id=1, source_target_pairs={{0,8},{2,10},{4,12},{6,14},{8,16},{10,18},{12,20},{14,22},{16,24},... | collective-permute-start | bytes 1572872 | tf_op jit(solution)/shard_map/ppermute | solution.py:15
  32.8 13.9 %collective-permute-start.9 = (bf16[128,2,1024]{0,2,1:T(8,128)(2,1)}, bf16[128,2,1024]{0,2,1:T(8,128)(2,1)S(1)}, u32[]{:S(2)}, u32[]{:S(2)}) collective-permute-start(bf16[128,2,1024]{0,2,1:T(8,128)(2,1)} %get-tuple-element.126), channel_id=1, source_target_pairs={{10,0},{12,2},{14,4},{16,6},{18,8},{20,10},{22,12},{24,14},{26,16}... | collective-permute-start | bytes 1572872 | tf_op jit(solution)/shard_map/ppermute | solution.py:15
  41.2 28.2 %collective-permute-start.3 = (bf16[128,2,1024]{0,2,1:T(8,128)(2,1)}, bf16[128,2,1024]{0,2,1:T(8,128)(2,1)S(1)}, u32[]{:S(2)}, u32[]{:S(2)}) collective-permute-start(bf16[128,2,1024]{0,2,1:T(8,128)(2,1)} %get-tuple-element.126), channel_id=1, source_target_pairs={{4,0},{6,2},{8,4},{10,6},{12,8},{14,10},{16,12},{18,14},{20,16},{2... | collective-permute-start | bytes 1572872 | tf_op jit(solution)/shard_map/ppermute | solution.py:15
  45.0 26.1 %collective-permute-start.1 = (bf16[128,2,1024]{0,2,1:T(8,128)(2,1)}, bf16[128,2,1024]{0,2,1:T(8,128)(2,1)S(1)}, u32[]{:S(2)}, u32[]{:S(2)}) collective-permute-start(bf16[128,2,1024]{0,2,1:T(8,128)(2,1)} %get-tuple-element.126), channel_id=1, source_target_pairs={{0,2},{2,4},{4,6},{6,8},{8,10},{10,12},{12,14},{14,16},{16,18},{18... | collective-permute-start | bytes 1572872 | tf_op jit(solution)/shard_map/ppermute | solution.py:15
  46.7 41.2 %collective-permute-start.5 = (bf16[128,4,1024]{0,2,1:T(8,128)(2,1)S(1)}, bf16[128,4,1024]{0,2,1:T(8,128)(2,1)S(1)}, u32[]{:S(2)}, u32[]{:S(2)}) collective-permute-start(bf16[128,4,1024]{0,2,1:T(8,128)(2,1)S(1)} %copy.35), channel_id=1, source_target_pairs={{6,0},{8,2},{10,4},{12,6},{14,8},{16,10},{18,12},{20,14},{22,16},{... | collective-permute-start | bytes 3145736 | tf_op jit(solution)/shard_map/ppermute | solution.py:15
  50.4 47.1 %collective-permute-start.4 = (bf16[128,4,1024]{0,2,1:T(8,128)(2,1)S(1)}, bf16[128,4,1024]{0,2,1:T(8,128)(2,1)S(1)}, u32[]{:S(2)}, u32[]{:S(2)}) collective-permute-start(bf16[128,4,1024]{0,2,1:T(8,128)(2,1)S(1)} %copy.35), channel_id=1, source_target_pairs={{0,6},{2,8},{4,10},{6,12},{8,14},{10,16},{12,18},{14,20},{16,22},{... | collective-permute-start | bytes 3145736 | tf_op jit(solution)/shard_map/ppermute | solution.py:15
  142.3 195.6 %reduce-scatter.4.cloned.1.call-start = ((), (), s32[]{:S(2)}) async-start(), calls=%async_computation.3 | async-start | bytes 3145728
  153.5 116.2 %collective-permute-start.18 = (bf16[128,2,1024]{0,2,1:T(8,128)(2,1)}, bf16[128,2,1024]{0,2,1:T(8,128)(2,1)S(1)}, u32[]{:S(2)}, u32[]{:S(2)}) collective-permute-start(bf16[128,2,1024]{0,2,1:T(8,128)(2,1)} %get-tuple-element.93), channel_id=1, source_target_pairs={{0,10},{2,12},{4,14},{6,16},{8,18},{10,20},{12,22},{14,24},{16,26}... | collective-permute-start | bytes 1572872 | tf_op jit(solution)/shard_map/ppermute | solution.py:15
  173.7 89.1 %collective-permute-start.16 = (bf16[128,2,1024]{0,2,1:T(8,128)(2,1)}, bf16[128,2,1024]{0,2,1:T(8,128)(2,1)S(1)}, u32[]{:S(2)}, u32[]{:S(2)}) collective-permute-start(bf16[128,2,1024]{0,2,1:T(8,128)(2,1)} %get-tuple-element.93), channel_id=1, source_target_pairs={{8,0},{10,2},{12,4},{14,6},{16,8},{18,10},{20,12},{22,14},{24,16},... | collective-permute-start | bytes 1572872 | tf_op jit(solution)/shard_map/ppermute | solution.py:15
  175.0 96.0 %collective-permute-start.19 = (bf16[128,2,1024]{0,2,1:T(8,128)(2,1)}, bf16[128,2,1024]{0,2,1:T(8,128)(2,1)S(1)}, u32[]{:S(2)}, u32[]{:S(2)}) collective-permute-start(bf16[128,2,1024]{0,2,1:T(8,128)(2,1)} %get-tuple-element.94), channel_id=1, source_target_pairs={{0,8},{2,10},{4,12},{6,14},{8,16},{10,18},{12,20},{14,22},{16,24},... | collective-permute-start | bytes 1572872 | tf_op jit(solution)/shard_map/ppermute | solution.py:15
  180.6 83.5 %collective-permute-start.17 = (bf16[128,2,1024]{0,2,1:T(8,128)(2,1)}, bf16[128,2,1024]{0,2,1:T(8,128)(2,1)S(1)}, u32[]{:S(2)}, u32[]{:S(2)}) collective-permute-start(bf16[128,2,1024]{0,2,1:T(8,128)(2,1)} %get-tuple-element.94), channel_id=1, source_target_pairs={{10,0},{12,2},{14,4},{16,6},{18,8},{20,10},{22,12},{24,14},{26,16}... | collective-permute-start | bytes 1572872 | tf_op jit(solution)/shard_map/ppermute | solution.py:15
  190.0 95.7 %collective-permute-start.12 = (bf16[128,2,1024]{0,2,1:T(8,128)(2,1)}, bf16[128,2,1024]{0,2,1:T(8,128)(2,1)}, u32[]{:S(2)}, u32[]{:S(2)}) collective-permute-start(bf16[128,2,1024]{0,2,1:T(8,128)(2,1)} %get-tuple-element.103), channel_id=1, source_target_pairs={{0,4},{2,6},{4,8},{6,10},{8,12},{10,14},{12,16},{14,18},{16,20},{1... | collective-permute-start | bytes 1572872 | tf_op jit(solution)/shard_map/ppermute | solution.py:15
  262.8 16.6 %collective-permute-start.10 = (bf16[128,2,1024]{0,2,1:T(8,128)(2,1)}, bf16[128,2,1024]{0,2,1:T(8,128)(2,1)S(1)}, u32[]{:S(2)}, u32[]{:S(2)}) collective-permute-start(bf16[128,2,1024]{0,2,1:T(8,128)(2,1)} %get-tuple-element.103), channel_id=1, source_target_pairs={{2,0},{4,2},{6,4},{8,6},{10,8},{12,10},{14,12},{16,14},{18,16},{20... | collective-permute-start | bytes 1572872 | tf_op jit(solution)/shard_map/ppermute | solution.py:15
  264.1 21.6 %collective-permute-start.13 = (bf16[128,2,1024]{0,2,1:T(8,128)(2,1)}, bf16[128,2,1024]{0,2,1:T(8,128)(2,1)S(1)}, u32[]{:S(2)}, u32[]{:S(2)}) collective-permute-start(bf16[128,2,1024]{0,2,1:T(8,128)(2,1)} %get-tuple-element.104), channel_id=1, source_target_pairs={{0,2},{2,4},{4,6},{6,8},{8,10},{10,12},{12,14},{14,16},{16,18},{18... | collective-permute-start | bytes 1572872 | tf_op jit(solution)/shard_map/ppermute | solution.py:15
  269.7 15.8 %collective-permute-start.11 = (bf16[128,2,1024]{0,2,1:T(8,128)(2,1)}, bf16[128,2,1024]{0,2,1:T(8,128)(2,1)S(1)}, u32[]{:S(2)}, u32[]{:S(2)}) collective-permute-start(bf16[128,2,1024]{0,2,1:T(8,128)(2,1)} %get-tuple-element.104), channel_id=1, source_target_pairs={{4,0},{6,2},{8,4},{10,6},{12,8},{14,10},{16,12},{18,14},{20,16},{2... | collective-permute-start | bytes 1572872 | tf_op jit(solution)/shard_map/ppermute | solution.py:15
  271.0 42.1 %collective-permute-start.15 = (bf16[128,4,1024]{0,2,1:T(8,128)(2,1)S(1)}, bf16[128,4,1024]{0,2,1:T(8,128)(2,1)S(1)}, u32[]{:S(2)}, u32[]{:S(2)}) collective-permute-start(bf16[128,4,1024]{0,2,1:T(8,128)(2,1)S(1)} %copy-done.54), channel_id=1, source_target_pairs={{0,6},{2,8},{4,10},{6,12},{8,14},{10,16},{12,18},{14,20},{16,22},{... | collective-permute-start | bytes 3145736 | tf_op jit(solution)/shard_map/ppermute | solution.py:15
  279.4 33.7 %collective-permute-start.14 = (bf16[128,4,1024]{0,2,1:T(8,128)(2,1)S(1)}, bf16[128,4,1024]{0,2,1:T(8,128)(2,1)S(1)}, u32[]{:S(2)}, u32[]{:S(2)}) collective-permute-start(bf16[128,4,1024]{0,2,1:T(8,128)(2,1)S(1)} %copy-done.54), channel_id=1, source_target_pairs={{6,0},{8,2},{10,4},{12,6},{14,8},{16,10},{18,12},{20,14},{22,16},{... | collective-permute-start | bytes 3145736 | tf_op jit(solution)/shard_map/ppermute | solution.py:15
  (105 other events, 1523.1 us)
Sparse Core Ops, SparseCore 0:
  26.4 32.4 all-gather.1
  142.4 116.8 all-reduce.1
  261.6 32.2 reduce-scatter.3
where the time goes:
time: 349 us; the launch traced here: 348 us
  waiting for transfers between devices  113 us (32%)
  starting transfers between devices  86.2 us (25%)
  other arithmetic  67.8 us (19%)
  local copies, waits for them, and re-layouts  58 us (17%)
  between operations  15.4 us (4%)
  matrix products  7.47 us (2%)
    ppermute x20, starting transfers between devices, shifted(): return lax.ppermute(block, axis, route)  86.1 us
    psum x1, waiting for transfers between devices, local(): flat = lax.psum(flat, 'band')  66.5 us
    ppermute x20, waiting for transfers between devices, shifted(): return lax.ppermute(block, axis, route)  46.3 us
    reduce_sum x4, other arithmetic, local(): jnp.sum(grad_f * jnp.roll(feat_rows[row_step * spacing], -col_step * spac...  21.7 us
    unnamed x220, local copies, waits for them, and re-layouts  20.7 us
    slice x18, local copies, waits for them, and re-layouts, local(): jnp.roll(grad_rows[-row_step * spacing], col_step * spacing, axis=-1)  17.5 us
    another operation x3, other arithmetic, local(): stacked = jnp.stack(branches)  17.2 us
    add x1, other arithmetic, local(): grad_input + kernel[which, tap_index][:, None, None] * jnp.roll(grad_rows...  15.6 us
  transfers between devices with their start and end apart: 23, of which 5 were waited for; matrix products, arithmetic and copies ran while one was open for 24% of the time, Pallas kernels for 0%

commit v1 on v0

--- a/solution.py
+++ b/solution.py
@@ -83,7 +83,9 @@
         depth_rows.append(jnp.stack(tap_rows))
     depth_local = jnp.stack(depth_rows)
     flat = jnp.concatenate([depth_local.reshape(-1), point_local.reshape(-1)])
-    flat = lax.psum(flat, "band")
+    flat = flat
+    for hop in (1, 2, 4, 8):
+        flat = flat + lax.ppermute(flat, "band", [(dev, dev ^ hop) for dev in range(16)])
     depth_total = flat[: depth_local.size].reshape(depth_local.shape)
     point_total = flat[depth_local.size :].reshape(point_local.shape)
     return (output, grad_input, depth_total / GSCALE, point_total / GSCALE)

time: 349 us -> 304 us (0.87)
  waiting for transfers between devices: 113 us -> 46.2 us
  starting transfers between devices: 86.2 us -> 118 us
  other arithmetic: 67.8 us -> 59.1 us
    psum x1 -> x0, waiting for transfers between devices: 66.5 us -> none  [local(): flat = lax.psum(flat, 'band')]
    ppermute x20, waiting for transfers between devices: 46.3 us -> 17.4 us  [shifted(): return lax.ppermute(block, axis, route)]
    ppermute x0 -> x4, waiting for transfers between devices: none -> 28.7 us  [local(): lax.ppermute(flat, 'band', [(dev, dev ^ hop) for dev in range(16)])]
    ppermute x0 -> x4, starting transfers between devices: none -> 28.3 us  [local(): lax.ppermute(flat, 'band', [(dev, dev ^ hop) for dev in range(16)])]
    another operation x3, local copies, waits for them, and re-layouts: 5.21 us -> 0.12 us  [local(): depth_rows.append(jnp.stack(tap_rows))]
    ppermute x20, starting transfers between devices: 86.1 us -> 90.1 us  [shifted(): return lax.ppermute(block, axis, route)]
    unnamed x220 -> x235, local copies, waits for them, and re-layouts: 20.7 us -> 22.5 us
  transfers between devices with their start and end apart: 23 -> 26, of which waited for: 5 -> 5; matrix products, arithmetic and copies ran while one was open for 24% -> 35% of each run, Pallas kernels for 0% -> 0%
where the time goes in v1:
time: 304 us; the launch traced here: 303 us
  starting transfers between devices  118 us (39%)
  other arithmetic  59.1 us (19%)
  local copies, waits for them, and re-layouts  56.4 us (19%)
  waiting for transfers between devices  46.2 us (15%)
  between operations  16 us (5%)
  matrix products  6.76 us (2%)
    ppermute x20, starting transfers between devices, shifted(): return lax.ppermute(block, axis, route)  90.1 us
    ppermute x4, waiting for transfers between devices, local(): lax.ppermute(flat, 'band', [(dev, dev ^ hop) for dev in range(16)])  28.7 us
    ppermute x4, starting transfers between devices, local(): lax.ppermute(flat, 'band', [(dev, dev ^ hop) for dev in range(16)])  28.3 us
    unnamed x235, local copies, waits for them, and re-layouts  22.5 us
    slice x18, local copies, waits for them, and re-layouts, local(): jnp.roll(grad_rows[-row_step * spacing], col_step * spacing, axis=-1)  20.6 us
    reduce_sum x4, other arithmetic, local(): jnp.sum(grad_f * jnp.roll(feat_rows[row_step * spacing], -col_step * spac...  19 us
    ppermute x20, waiting for transfers between devices, shifted(): return lax.ppermute(block, axis, route)  17.4 us
    add x1, other arithmetic, local(): grad_input + kernel[which, tap_index][:, None, None] * jnp.roll(grad_rows...  15.9 us
  transfers between devices with their start and end apart: 26, of which 5 were waited for; matrix products, arithmetic and copies ran while one was open for 35% of the time, Pallas kernels for 0%

profile of v1, /device:TPU:0, one launch (start us, length us, event | category | flops | bytes accessed | tf_op | source)
XLA Modules:
  0.0 302.8 jit_solution(15299002375751624634)
XLA Ops:
  11.5 5.1 %collective-permute-start.6 = (bf16[128,2,1024]{0,2,1:T(8,128)(2,1)}, bf16[128,2,1024]{0,2,1:T(8,128)(2,1)S(1)}, u32[]{:S(2)}, u32[]{:S(2)}) collective-permute-start(bf16[128,2,1024]{0,2,1:T(8,128)(2,1)} %get-tuple-element.125), channel_id=1, source_target_pairs={{0,10},{2,12},{4,14},{6,16},{8,18},{10,20},{12,22},{14,24},{16,26}... | collective-permute-start | bytes 1572872 | tf_op jit(solution)/shard_map/ppermute | solution.py:15
  17.9 7.0 %collective-permute-start = (bf16[128,2,1024]{0,2,1:T(8,128)(2,1)}, bf16[128,2,1024]{0,2,1:T(8,128)(2,1)}, u32[]{:S(2)}, u32[]{:S(2)}) collective-permute-start(bf16[128,2,1024]{0,2,1:T(8,128)(2,1)} %get-tuple-element.125), channel_id=1, source_target_pairs={{0,4},{2,6},{4,8},{6,10},{8,12},{10,14},{12,16},{14,18},{16,20},{1... | collective-permute-start | bytes 1572872 | tf_op jit(solution)/shard_map/ppermute | solution.py:15
  33.9 7.3 %collective-permute-done.7 = bf16[128,2,1024]{0,2,1:T(8,128)(2,1)S(1)} collective-permute-done((bf16[128,2,1024]{0,2,1:T(8,128)(2,1)}, bf16[128,2,1024]{0,2,1:T(8,128)(2,1)S(1)}, u32[]{:S(2)}, u32[]{:S(2)}) %collective-permute-start.7) | collective-permute-done | bytes 524320 | tf_op jit(solution)/shard_map/ppermute | solution.py:15
  50.4 19.1 %collective-permute-start.4 = (bf16[128,4,1024]{0,2,1:T(8,128)(2,1)S(1)}, bf16[128,4,1024]{0,2,1:T(8,128)(2,1)S(1)}, u32[]{:S(2)}, u32[]{:S(2)}) collective-permute-start(bf16[128,4,1024]{0,2,1:T(8,128)(2,1)S(1)} %copy.35), channel_id=1, source_target_pairs={{0,6},{2,8},{4,10},{6,12},{8,14},{10,16},{12,18},{14,20},{16,22},{... | collective-permute-start | bytes 3145736 | tf_op jit(solution)/shard_map/ppermute | solution.py:15
  75.3 6.8 %fusion.75 = bf16[1,128,4,1024]{1,3,0,2:T(8,128)(2,1)} fusion(f32[128,4,18]{0,2,1:T(8,128)S(1)} %get-tuple-element.90, f32[128,4,1006]{0,2,1:T(8,128)} %get-tuple-element.92, f32[128]{0:T(128)S(1)} %get-tuple-element.128, f32[128]{0:T(128)S(1)} %get-tuple-element.129, f32[128,4,1006]{0,2,1:T(8,128)} %get-tuple-element.91, ...), kind=kLoop, calls=%fused_computation.159 | loop fusion | flops 15204352 | bytes 16781824 | tf_op jit(solution)/shard_map/stack | solution.py:49
  82.2 5.0 %fusion.77 = bf16[1,128,4,1024]{1,3,0,2:T(8,128)(2,1)S(1)} fusion(f32[128,4,6]{0,2,1:T(8,128)S(1)} %get-tuple-element.82, f32[128,4,1018]{0,2,1:T(8,128)S(1)} %get-tuple-element.84, f32[128]{0:T(128)} %get-tuple-element.147, f32[128]{0:T(128)} %get-tuple-element.148, f32[128,4,1018]{0,2,1:T(8,128)S(1)} %get-tuple-element.83, ...), kind=kLoop, calls=%fused_computation.161 | loop fusion | flops 15204352 | bytes 16781824 | tf_op jit(solution)/shard_map/stack | solution.py:49
  87.4 10.1 %collective-permute-done.4 = bf16[128,4,1024]{0,2,1:T(8,128)(2,1)S(1)} collective-permute-done((bf16[128,4,1024]{0,2,1:T(8,128)(2,1)S(1)}, bf16[128,4,1024]{0,2,1:T(8,128)(2,1)S(1)}, u32[]{:S(2)}, u32[]{:S(2)}) %collective-permute-start.4) | collective-permute-done | bytes 1048608 | tf_op jit(solution)/shard_map/ppermute | solution.py:15
  104.6 4.1 %copy.56 = bf16[256,4096]{1,0:T(8,128)(2,1)} copy(bf16[256,4096]{0,1:T(8,128)(2,1)} %bitcast.200) | data formatting | bytes 4194304
  108.8 3.0 %convolution_convert_fusion = bf16[4,128,4,1024]{1,3,2,0:T(8,128)(2,1)S(1)} fusion(bf16[256,4,1024]{2,0,1:T(8,128)(2,1)} %all-gather.2.cloned.1.call-done, bf16[4,128,256]{2,1,0:T(8,128)(2,1)S(1)} %copy-done), kind=kOutput, calls=%fused_computation.35 | convolution fusion | flops 1075838976 | bytes 6553600 | tf_op jit(solution)/shard_map/bco,ohw->bchw/dot_general | solution.py:59
  112.3 5.2 %fusion.47 = (f32[128]{0:T(128)S(1)}, f32[128]{0:T(128)S(1)}, f32[128]{0:T(128)S(1)}, f32[128]{0:T(128)S(1)}, f32[128]{0:T(128)S(1)}, /*index=5*/f32[128]{0:T(128)S(1)}) fusion(f32[128,4,1018]{0,2,1:T(8,128)S(1)} %copy-done.16, f32[128,4,6]{0,2,1:T(8,128)S(1)} %copy-done.89, bf16[4,128,4,1024]{1,3,2,0:T(8,128)(2,1)S(1)} %convolution_convert_fusion, ...), kind=kLoop, calls=%fused_computation.83 | loop fusion | flops 10484992 | bytes 14683136 | tf_op jit(solution)/shard_map/reduce_sum | solution.py:78
  121.2 20.4 %collective-permute-start.18 = (bf16[128,2,1024]{0,2,1:T(8,128)(2,1)}, bf16[128,2,1024]{0,2,1:T(8,128)(2,1)}, u32[]{:S(2)}, u32[]{:S(2)}) collective-permute-start(bf16[128,2,1024]{0,2,1:T(8,128)(2,1)} %get-tuple-element.93), channel_id=1, source_target_pairs={{0,10},{2,12},{4,14},{6,16},{8,18},{10,20},{12,22},{14,24},{16,26}... | collective-permute-start | bytes 1572872 | tf_op jit(solution)/shard_map/ppermute | solution.py:15
  142.9 6.3 %collective-permute-start.19 = (bf16[128,2,1024]{0,2,1:T(8,128)(2,1)}, bf16[128,2,1024]{0,2,1:T(8,128)(2,1)}, u32[]{:S(2)}, u32[]{:S(2)}) collective-permute-start(bf16[128,2,1024]{0,2,1:T(8,128)(2,1)} %get-tuple-element.94), channel_id=1, source_target_pairs={{0,8},{2,10},{4,12},{6,14},{8,16},{10,18},{12,20},{14,22},{16,24},... | collective-permute-start | bytes 1572872 | tf_op jit(solution)/shard_map/ppermute | solution.py:15
  159.1 3.9 %fusion.48 = (f32[128]{0:T(128)S(1)}, f32[128]{0:T(128)S(1)}, f32[128]{0:T(128)S(1)}, f32[128]{0:T(128)S(1)}, f32[128]{0:T(128)S(1)}, /*index=5*/f32[128]{0:T(128)S(1)}, f32[128]{0:T(128)S(1)}) fusion(bf16[128,2,1024]{0,2,1:T(8,128)(2,1)S(1)} %copy-done.44, bf16[128,2,1024]{0,2,1:T(8,128)(2,1)} %collective-permute-done.2, ...), kind=kLoop, calls=%fused_computation.84 | loop fusion | flops 13630592 | bytes 13635072 | tf_op jit(solution)/shard_map/reduce_sum | solution.py:78
  163.1 4.1 %fusion.45 = (f32[128]{0:T(128)S(1)}, f32[128]{0:T(128)S(1)}, f32[128]{0:T(128)S(1)}, f32[128]{0:T(128)S(1)}, f32[128]{0:T(128)S(1)}, /*index=5*/f32[128]{0:T(128)S(1)}, f32[128]{0:T(128)S(1)}, f32[128]{0:T(128)S(1)}) fusion(bf16[128,4,1024]{0,2,1:T(8,128)(2,1)S(1)} %copy.35, bf16[4,128,4,1024]{1,3,2,0:T(8,128)(2,1)S(1)} %convolution_convert_fusion, ...), kind=kLoop, calls=%fused_computation.81 | loop fusion | flops 13630464 | bytes 13635584 | tf_op jit(solution)/shard_map/reduce_sum | solution.py:78
  167.3 5.8 %fusion.49 = (f32[128]{0:T(128)S(1)}, f32[128]{0:T(128)S(1)}, f32[128]{0:T(128)S(1)}, f32[128]{0:T(128)S(1)}, f32[128]{0:T(128)S(1)}, /*index=5*/f32[128]{0:T(128)S(1)}) fusion(f32[128,4,6]{0,2,1:T(8,128)S(1)} %copy-done.83, f32[128,4,1018]{0,2,1:T(8,128)S(1)} %copy-done.14, bf16[4,128,4,1024]{1,3,2,0:T(8,128)(2,1)} %copy-done.2, ...), kind=kLoop, calls=%fused_computation.85 | loop fusion | flops 11009280 | bytes 13634560 | tf_op jit(solution)/shard_map/reduce_sum | solution.py:78
  183.1 4.8 %collective-permute-start.13 = (bf16[128,2,1024]{0,2,1:T(8,128)(2,1)S(1)}, bf16[128,2,1024]{0,2,1:T(8,128)(2,1)S(1)}, u32[]{:S(2)}, u32[]{:S(2)}) collective-permute-start(bf16[128,2,1024]{0,2,1:T(8,128)(2,1)S(1)} %get-tuple-element.104), channel_id=1, source_target_pairs={{0,2},{2,4},{4,6},{6,8},{8,10},{10,12},{12,14},{14,16},{16,18},{18... | collective-permute-start | bytes 1572872 | tf_op jit(solution)/shard_map/ppermute | solution.py:15
  190.6 8.2 %collective-permute-start.15 = (bf16[128,4,1024]{0,2,1:T(8,128)(2,1)S(1)}, bf16[128,4,1024]{0,2,1:T(8,128)(2,1)S(1)}, u32[]{:S(2)}, u32[]{:S(2)}) collective-permute-start(bf16[128,4,1024]{0,2,1:T(8,128)(2,1)S(1)} %copy-done.51), channel_id=1, source_target_pairs={{0,6},{2,8},{4,10},{6,12},{8,14},{10,16},{12,18},{14,20},{16,22},{... | collective-permute-start | bytes 3145736 | tf_op jit(solution)/shard_map/ppermute | solution.py:15
  204.0 20.5 %collective-permute-start.20 = (f32[134528]{0:T(1024)S(1)}, f32[134528]{0:T(1024)S(1)}, u32[]{:S(2)}, u32[]{:S(2)}) collective-permute-start(f32[134528]{0:T(1024)S(1)} %constant_dynamic-update-slice_fusion), channel_id=1, source_target_pairs={{0,2},{2,0},{4,6},{6,4},{8,10},{10,8},{12,14},{14,12},{16,18},{18,... | collective-permute-start | bytes 1614344 | tf_op jit(solution)/shard_map/ppermute | solution.py:88
  229.3 2.9 collective-permute-start.21
  235.3 11.3 %collective-permute-done.21 = f32[134528]{0:T(1024)S(1)} collective-permute-done((f32[134528]{0:T(1024)S(1)}, f32[134528]{0:T(1024)S(1)}, u32[]{:S(2)}, u32[]{:S(2)}) %collective-permute-start.21) | collective-permute-done | bytes 538144 | tf_op jit(solution)/shard_map/ppermute | solution.py:88
  246.6 4.7 %collective-permute-start.22 = (f32[134528]{0:T(1024)S(1)}, f32[134528]{0:T(1024)S(1)}, u32[]{:S(2)}, u32[]{:S(2)}) collective-permute-start(f32[134528]{0:T(1024)S(1)} %add.219), channel_id=1, source_target_pairs={{0,8},{2,10},{4,12},{6,14},{8,0},{10,2},{12,4},{14,6},{16,24},{18,... | collective-permute-start | bytes 1614344 | tf_op jit(solution)/shard_map/ppermute | solution.py:88
  254.4 9.3 %collective-permute-done.22 = f32[134528]{0:T(1024)S(1)} collective-permute-done((f32[134528]{0:T(1024)S(1)}, f32[134528]{0:T(1024)S(1)}, u32[]{:S(2)}, u32[]{:S(2)}) %collective-permute-start.22) | collective-permute-done | bytes 538144 | tf_op jit(solution)/shard_map/ppermute | solution.py:88
  263.9 15.9 %fusion.40 = f32[128,4,1024]{0,2,1:T(8,128)S(1)} fusion(f32[128,4,6]{0,2,1:T(8,128)} %get-tuple-element.74, f32[128,4,1018]{0,2,1:T(8,128)S(1)} %get-tuple-element.76, f32[128,4,1018]{0,2,1:T(8,128)S(1)} %get-tuple-element.75, f32[128,4,6]{0,2,1:T(8,128)} %get-tuple-element.73, f32[128,4,6]{0,2,1:T(8,128)S(1)} %copy-done.92, ...), kind=kLoop, calls=%fused_computation.76 | loop fusion | flops 45088768 | bytes 50345472 | tf_op jit(solution)/shard_map/add | solution.py:74
  281.8 8.1 %collective-permute-done.23 = f32[134528]{0:T(1024)} collective-permute-done((f32[134528]{0:T(1024)S(1)}, f32[134528]{0:T(1024)}, u32[]{:S(2)}, u32[]{:S(2)}) %collective-permute-start.23) | collective-permute-done | bytes 538144 | tf_op jit(solution)/shard_map/ppermute | solution.py:88
  (342 shorter events, 87.9 us)
Async XLA Ops:
  7.2 101.5 %all-gather.2.cloned.1.call-start = ((), (), s32[]{:S(2)}) async-start(), calls=%async_computation.1 | async-start | bytes 3145728 | tf_op jit(solution)/shard_map/all_gather | solution.py:58
  10.3 34.6 %collective-permute-start.8 = (bf16[128,2,1024]{0,2,1:T(8,128)(2,1)}, bf16[128,2,1024]{0,2,1:T(8,128)(2,1)S(1)}, u32[]{:S(2)}, u32[]{:S(2)}) collective-permute-start(bf16[128,2,1024]{0,2,1:T(8,128)(2,1)} %get-tuple-element.125), channel_id=1, source_target_pairs={{8,0},{10,2},{12,4},{14,6},{16,8},{18,10},{20,12},{22,14},{24,16},... | collective-permute-start | bytes 1572872 | tf_op jit(solution)/shard_map/ppermute | solution.py:15
  11.5 21.1 %collective-permute-start.6 = (bf16[128,2,1024]{0,2,1:T(8,128)(2,1)}, bf16[128,2,1024]{0,2,1:T(8,128)(2,1)S(1)}, u32[]{:S(2)}, u32[]{:S(2)}) collective-permute-start(bf16[128,2,1024]{0,2,1:T(8,128)(2,1)} %get-tuple-element.125), channel_id=1, source_target_pairs={{0,10},{2,12},{4,14},{6,16},{8,18},{10,20},{12,22},{14,24},{16,26}... | collective-permute-start | bytes 1572872 | tf_op jit(solution)/shard_map/ppermute | solution.py:15
  16.6 33.7 %collective-permute-start.2 = (bf16[128,2,1024]{0,2,1:T(8,128)(2,1)}, bf16[128,2,1024]{0,2,1:T(8,128)(2,1)}, u32[]{:S(2)}, u32[]{:S(2)}) collective-permute-start(bf16[128,2,1024]{0,2,1:T(8,128)(2,1)} %get-tuple-element.125), channel_id=1, source_target_pairs={{2,0},{4,2},{6,4},{8,6},{10,8},{12,10},{14,12},{16,14},{18,16},{20... | collective-permute-start | bytes 1572872 | tf_op jit(solution)/shard_map/ppermute | solution.py:15
  17.9 53.3 %collective-permute-start = (bf16[128,2,1024]{0,2,1:T(8,128)(2,1)}, bf16[128,2,1024]{0,2,1:T(8,128)(2,1)}, u32[]{:S(2)}, u32[]{:S(2)}) collective-permute-start(bf16[128,2,1024]{0,2,1:T(8,128)(2,1)} %get-tuple-element.125), channel_id=1, source_target_pairs={{0,4},{2,6},{4,8},{6,10},{8,12},{10,14},{12,16},{14,18},{16,20},{1... | collective-permute-start | bytes 1572872 | tf_op jit(solution)/shard_map/ppermute | solution.py:15
  26.2 266.4 %reduce-scatter.4.cloned.1.call-start = ((), (), s32[]{:S(2)}) async-start(), calls=%async_computation.2 | async-start | bytes 3145728
  41.2 28.3 %collective-permute-start.3 = (bf16[128,2,1024]{0,2,1:T(8,128)(2,1)}, bf16[128,2,1024]{0,2,1:T(8,128)(2,1)S(1)}, u32[]{:S(2)}, u32[]{:S(2)}) collective-permute-start(bf16[128,2,1024]{0,2,1:T(8,128)(2,1)} %get-tuple-element.126), channel_id=1, source_target_pairs={{4,0},{6,2},{8,4},{10,6},{12,8},{14,10},{16,12},{18,14},{20,16},{2... | collective-permute-start | bytes 1572872 | tf_op jit(solution)/shard_map/ppermute | solution.py:15
  44.9 26.3 %collective-permute-start.1 = (bf16[128,2,1024]{0,2,1:T(8,128)(2,1)}, bf16[128,2,1024]{0,2,1:T(8,128)(2,1)S(1)}, u32[]{:S(2)}, u32[]{:S(2)}) collective-permute-start(bf16[128,2,1024]{0,2,1:T(8,128)(2,1)} %get-tuple-element.126), channel_id=1, source_target_pairs={{0,2},{2,4},{4,6},{6,8},{8,10},{10,12},{12,14},{14,16},{16,18},{18... | collective-permute-start | bytes 1572872 | tf_op jit(solution)/shard_map/ppermute | solution.py:15
  46.6 40.7 %collective-permute-start.5 = (bf16[128,4,1024]{0,2,1:T(8,128)(2,1)S(1)}, bf16[128,4,1024]{0,2,1:T(8,128)(2,1)S(1)}, u32[]{:S(2)}, u32[]{:S(2)}) collective-permute-start(bf16[128,4,1024]{0,2,1:T(8,128)(2,1)S(1)} %copy.35), channel_id=1, source_target_pairs={{6,0},{8,2},{10,4},{12,6},{14,8},{16,10},{18,12},{20,14},{22,16},{... | collective-permute-start | bytes 3145736 | tf_op jit(solution)/shard_map/ppermute | solution.py:15
  50.4 47.1 %collective-permute-start.4 = (bf16[128,4,1024]{0,2,1:T(8,128)(2,1)S(1)}, bf16[128,4,1024]{0,2,1:T(8,128)(2,1)S(1)}, u32[]{:S(2)}, u32[]{:S(2)}) collective-permute-start(bf16[128,4,1024]{0,2,1:T(8,128)(2,1)S(1)} %copy.35), channel_id=1, source_target_pairs={{0,6},{2,8},{4,10},{6,12},{8,14},{10,16},{12,18},{14,20},{16,22},{... | collective-permute-start | bytes 3145736 | tf_op jit(solution)/shard_map/ppermute | solution.py:15
  121.2 68.1 %collective-permute-start.18 = (bf16[128,2,1024]{0,2,1:T(8,128)(2,1)}, bf16[128,2,1024]{0,2,1:T(8,128)(2,1)}, u32[]{:S(2)}, u32[]{:S(2)}) collective-permute-start(bf16[128,2,1024]{0,2,1:T(8,128)(2,1)} %get-tuple-element.93), channel_id=1, source_target_pairs={{0,10},{2,12},{4,14},{6,16},{8,18},{10,20},{12,22},{14,24},{16,26}... | collective-permute-start | bytes 1572872 | tf_op jit(solution)/shard_map/ppermute | solution.py:15
  141.6 40.1 %collective-permute-start.16 = (bf16[128,2,1024]{0,2,1:T(8,128)(2,1)}, bf16[128,2,1024]{0,2,1:T(8,128)(2,1)}, u32[]{:S(2)}, u32[]{:S(2)}) collective-permute-start(bf16[128,2,1024]{0,2,1:T(8,128)(2,1)} %get-tuple-element.93), channel_id=1, source_target_pairs={{8,0},{10,2},{12,4},{14,6},{16,8},{18,10},{20,12},{22,14},{24,16},... | collective-permute-start | bytes 1572872 | tf_op jit(solution)/shard_map/ppermute | solution.py:15
  142.9 47.7 %collective-permute-start.19 = (bf16[128,2,1024]{0,2,1:T(8,128)(2,1)}, bf16[128,2,1024]{0,2,1:T(8,128)(2,1)}, u32[]{:S(2)}, u32[]{:S(2)}) collective-permute-start(bf16[128,2,1024]{0,2,1:T(8,128)(2,1)} %get-tuple-element.94), channel_id=1, source_target_pairs={{0,8},{2,10},{4,12},{6,14},{8,16},{10,18},{12,20},{14,22},{16,24},... | collective-permute-start | bytes 1572872 | tf_op jit(solution)/shard_map/ppermute | solution.py:15
  149.2 33.9 %collective-permute-start.17 = (bf16[128,2,1024]{0,2,1:T(8,128)(2,1)}, bf16[128,2,1024]{0,2,1:T(8,128)(2,1)}, u32[]{:S(2)}, u32[]{:S(2)}) collective-permute-start(bf16[128,2,1024]{0,2,1:T(8,128)(2,1)} %get-tuple-element.94), channel_id=1, source_target_pairs={{10,0},{12,2},{14,4},{16,6},{18,8},{20,10},{22,12},{24,14},{26,16}... | collective-permute-start | bytes 1572872 | tf_op jit(solution)/shard_map/ppermute | solution.py:15
  174.6 27.8 %collective-permute-start.12 = (bf16[128,2,1024]{0,2,1:T(8,128)(2,1)S(1)}, bf16[128,2,1024]{0,2,1:T(8,128)(2,1)S(1)}, u32[]{:S(2)}, u32[]{:S(2)}) collective-permute-start(bf16[128,2,1024]{0,2,1:T(8,128)(2,1)S(1)} %get-tuple-element.103), channel_id=1, source_target_pairs={{0,4},{2,6},{4,8},{6,10},{8,12},{10,14},{12,16},{14,18},{16,20},{1... | collective-permute-start | bytes 1572872 | tf_op jit(solution)/shard_map/ppermute | solution.py:15
  181.7 45.7 %collective-permute-start.10 = (bf16[128,2,1024]{0,2,1:T(8,128)(2,1)S(1)}, bf16[128,2,1024]{0,2,1:T(8,128)(2,1)S(1)}, u32[]{:S(2)}, u32[]{:S(2)}) collective-permute-start(bf16[128,2,1024]{0,2,1:T(8,128)(2,1)S(1)} %get-tuple-element.103), channel_id=1, source_target_pairs={{2,0},{4,2},{6,4},{8,6},{10,8},{12,10},{14,12},{16,14},{18,16},{20... | collective-permute-start | bytes 1572872 | tf_op jit(solution)/shard_map/ppermute | solution.py:15
  183.1 20.8 %collective-permute-start.13 = (bf16[128,2,1024]{0,2,1:T(8,128)(2,1)S(1)}, bf16[128,2,1024]{0,2,1:T(8,128)(2,1)S(1)}, u32[]{:S(2)}, u32[]{:S(2)}) collective-permute-start(bf16[128,2,1024]{0,2,1:T(8,128)(2,1)S(1)} %get-tuple-element.104), channel_id=1, source_target_pairs={{0,2},{2,4},{4,6},{6,8},{8,10},{10,12},{12,14},{14,16},{16,18},{18... | collective-permute-start | bytes 1572872 | tf_op jit(solution)/shard_map/ppermute | solution.py:15
  189.3 38.1 %collective-permute-start.11 = (bf16[128,2,1024]{0,2,1:T(8,128)(2,1)S(1)}, bf16[128,2,1024]{0,2,1:T(8,128)(2,1)S(1)}, u32[]{:S(2)}, u32[]{:S(2)}) collective-permute-start(bf16[128,2,1024]{0,2,1:T(8,128)(2,1)S(1)} %get-tuple-element.104), channel_id=1, source_target_pairs={{4,0},{6,2},{8,4},{10,6},{12,8},{14,10},{16,12},{18,14},{20,16},{2... | collective-permute-start | bytes 1572872 | tf_op jit(solution)/shard_map/ppermute | solution.py:15
  190.6 60.7 %collective-permute-start.15 = (bf16[128,4,1024]{0,2,1:T(8,128)(2,1)S(1)}, bf16[128,4,1024]{0,2,1:T(8,128)(2,1)S(1)}, u32[]{:S(2)}, u32[]{:S(2)}) collective-permute-start(bf16[128,4,1024]{0,2,1:T(8,128)(2,1)S(1)} %copy-done.51), channel_id=1, source_target_pairs={{0,6},{2,8},{4,10},{6,12},{8,14},{10,16},{12,18},{14,20},{16,22},{... | collective-permute-start | bytes 3145736 | tf_op jit(solution)/shard_map/ppermute | solution.py:15
  202.4 29.9 %collective-permute-start.14 = (bf16[128,4,1024]{0,2,1:T(8,128)(2,1)S(1)}, bf16[128,4,1024]{0,2,1:T(8,128)(2,1)S(1)}, u32[]{:S(2)}, u32[]{:S(2)}) collective-permute-start(bf16[128,4,1024]{0,2,1:T(8,128)(2,1)S(1)} %copy-done.51), channel_id=1, source_target_pairs={{6,0},{8,2},{10,4},{12,6},{14,8},{16,10},{18,12},{20,14},{22,16},{... | collective-permute-start | bytes 3145736 | tf_op jit(solution)/shard_map/ppermute | solution.py:15
  204.0 25.3 %collective-permute-start.20 = (f32[134528]{0:T(1024)S(1)}, f32[134528]{0:T(1024)S(1)}, u32[]{:S(2)}, u32[]{:S(2)}) collective-permute-start(f32[134528]{0:T(1024)S(1)} %constant_dynamic-update-slice_fusion), channel_id=1, source_target_pairs={{0,2},{2,0},{4,6},{6,4},{8,10},{10,8},{12,14},{14,12},{16,18},{18,... | collective-permute-start | bytes 1614344 | tf_op jit(solution)/shard_map/ppermute | solution.py:88
  229.3 17.2 %collective-permute-start.21 = (f32[134528]{0:T(1024)S(1)}, f32[134528]{0:T(1024)S(1)}, u32[]{:S(2)}, u32[]{:S(2)}) collective-permute-start(f32[134528]{0:T(1024)S(1)} %add.218), channel_id=1, source_target_pairs={{0,4},{2,6},{4,0},{6,2},{8,12},{10,14},{12,8},{14,10},{16,20},{18,... | collective-permute-start | bytes 1614344 | tf_op jit(solution)/shard_map/ppermute | solution.py:88
  246.6 17.1 %collective-permute-start.22 = (f32[134528]{0:T(1024)S(1)}, f32[134528]{0:T(1024)S(1)}, u32[]{:S(2)}, u32[]{:S(2)}) collective-permute-start(f32[134528]{0:T(1024)S(1)} %add.219), channel_id=1, source_target_pairs={{0,8},{2,10},{4,12},{6,14},{8,0},{10,2},{12,4},{14,6},{16,24},{18,... | collective-permute-start | bytes 1614344 | tf_op jit(solution)/shard_map/ppermute | solution.py:88
  263.7 26.2 %collective-permute-start.23 = (f32[134528]{0:T(1024)S(1)}, f32[134528]{0:T(1024)}, u32[]{:S(2)}, u32[]{:S(2)}) collective-permute-start(f32[134528]{0:T(1024)S(1)} %add.220), channel_id=1, source_target_pairs={{0,16},{2,18},{4,20},{6,22},{8,24},{10,26},{12,28},{14,30},{16,0},... | collective-permute-start | bytes 1614344 | tf_op jit(solution)/shard_map/ppermute | solution.py:88
  (115 other events, 1729.3 us)
Sparse Core Ops, SparseCore 0:
  26.3 32.4 all-gather.1
  108.8 51.2 reduce-scatter.3
